TPU v7x, 256 devices: a whole 4x4x8 slice. The times are simulated.
256 devices in a mesh: dp: 4 (over x), seq: 4 (over y_hi, core), tensor: 16 (over y_lo, z).
Axes of the slice: x: 4, y: 4 (y_hi: 2, y_lo: 2; y = y_hi * 2 + y_lo), z: 8, core: 2. Of those that a mesh axis runs over, the one named last changes fastest.
Arguments:
- byte_acts: bfloat16 [4, 16384, 2048], P('dp', 'seq', 'tensor'), may hold values from -18 to 18
- conv_weight: bfloat16 [16, 1024, 128], P('tensor'), may hold values from -0.1875 to 0.1875
- conv_bias: float32 [2048], P('tensor'), may hold values from -3 to 3
- proj_weight: bfloat16 [2048, 8192], P(None, 'tensor'), may hold values from -0.125 to 0.125
- teacher: bfloat16 [4, 4096, 8192], P('dp', 'seq', 'tensor'), may hold values from -6 to 6
- span_lengths: int32 [4, 4096], P('dp'), may hold values from 1 to 16, as said below
Outputs:
- downsampled: bfloat16 [4, 4096, 2048], P('dp', 'seq', 'tensor')
- byte_grad: bfloat16 [4, 16384, 2048], P('dp', 'seq', 'tensor')
- conv_grad: float32 [16, 1024, 128], P('tensor')
- proj_grad: float32 [2048, 8192], P(None, 'tensor')
Inputs may be any that keep to these rules, and one draw needn't show every extreme that they name: `span_lengths`: each document's 4096 span lengths cover its 16384 bytes in order; the longest is exactly 16.
All inputs are finite; a program needn't handle non-finite values.
Results may differ from a plain program's by a relative error of at most 0.019.
Values may be sent and summed in bfloat16 or wider, within the bound.
No kernel may reach another device: no remote copies, remote signals or barrier semaphores. Data moves between devices by JAX's collectives and lax.ppermute only.
A program may use at most 64 MiB of HBM per device.

v0:
```python
import jax
import jax.numpy as jnp
from jax import lax
from jax.sharding import PartitionSpec as P

STRIDE = 4
KERNEL = 8


def shifted(block, axis, distance):
    devices = range(lax.axis_size(axis))
    route = [(i - distance, i) for i in devices if i - distance in devices]
    return lax.ppermute(block, axis, route)


def intersection_weights(span_start, span_end, span_lengths, first_position, position_count):
    byte_first = (first_position + jnp.arange(position_count, dtype=jnp.int32)) * STRIDE
    lower_edge = jnp.maximum(span_start[:, None], byte_first[None, :])
    upper_edge = jnp.minimum(span_end[:, None], byte_first[None, :] + STRIDE)
    covered = jnp.maximum(upper_edge - lower_edge, 0).astype(jnp.float32)
    return (covered / span_lengths[:, None].astype(jnp.float32)).astype(jnp.bfloat16)


def local(byte_acts, conv_weight, conv_bias, proj_weight, teacher, span_lengths):
    byte_rows = byte_acts[0]
    row_total, width = byte_rows.shape
    groups_here = conv_weight.shape[0]
    group_width = width // groups_here
    positions = row_total // STRIDE
    seq_count = lax.axis_size("seq")
    seq_rank = lax.axis_index("seq")
    lengths_doc = span_lengths[0]
    tokens_all = lengths_doc.shape[0]
    span_end = jnp.cumsum(lengths_doc)
    span_start = span_end - lengths_doc
    next_rows = shifted(byte_rows[:STRIDE], "seq", -1)
    extended = jnp.concatenate([byte_rows, next_rows], axis=0)
    blocks = extended.reshape(positions + 1, STRIDE, groups_here, group_width)
    windows = jnp.concatenate([blocks[:-1], blocks[1:]], axis=1)
    taps_weight = conv_weight.reshape(groups_here, KERNEL, group_width, group_width)
    conv_out = jnp.einsum(
        "pkgc,gkco->pgo", windows, taps_weight, preferred_element_type=jnp.float32
    )
    conv_out = conv_out + conv_bias.reshape(groups_here, group_width)[None]
    downsampled = conv_out.reshape(positions, width).astype(jnp.bfloat16)
    local_weight = intersection_weights(
        span_start, span_end, lengths_doc, seq_rank * positions, positions
    )
    weight_part = local_weight
    pooled_sum = lax.psum_scatter(
        jnp.dot(weight_part, downsampled, preferred_element_type=jnp.float32).astype(jnp.bfloat16),
        "seq",
        scatter_dimension=0,
        tiled=True,
    )
    gathered = lax.all_gather(pooled_sum, "tensor", axis=1, tiled=True)
    predicted = jnp.dot(gathered, proj_weight, preferred_element_type=jnp.float32)
    err_grad = (predicted - teacher[0].astype(jnp.float32)).astype(jnp.bfloat16)
    proj_local = lax.dot_general(
        gathered, err_grad, (((0,), (0,)), ((), ())), preferred_element_type=jnp.float32
    )
    token_scale = 1.0 / jnp.sqrt(jnp.float32(lax.axis_size("dp") * tokens_all))
    proj_summed = lax.psum(proj_local.astype(jnp.bfloat16), ("dp", "seq")).astype(jnp.float32)
    proj_grad = proj_summed * token_scale
    weight_part = proj_weight
    pooled_grad_t = lax.psum_scatter(
        lax.dot_general(
            weight_part, err_grad, (((1,), (1,)), ((), ())), preferred_element_type=jnp.float32
        ).astype(jnp.bfloat16),
        "tensor",
        scatter_dimension=0,
        tiled=True,
    )
    weight_part = local_weight
    down_sum = lax.dot_general(
        weight_part,
        lax.all_gather(pooled_grad_t, "seq", axis=1, tiled=True),
        (((0,), (1,)), ((), ())),
        preferred_element_type=jnp.float32,
    )
    down_grad = down_sum.astype(jnp.bfloat16).reshape(positions, groups_here, group_width)
    conv_local = jnp.einsum(
        "pkgc,pgo->gkco", windows, down_grad, preferred_element_type=jnp.float32
    )
    conv_summed = lax.psum(conv_local.astype(jnp.bfloat16), ("dp", "seq")).astype(jnp.float32)
    position_scale = 1.0 / jnp.sqrt(jnp.float32(lax.axis_size("dp") * positions * seq_count))
    conv_grad = (conv_summed * position_scale).reshape(
        groups_here, KERNEL * group_width, group_width
    )
    window_grad = jnp.einsum(
        "pgo,gkco->pkgc", down_grad, taps_weight, preferred_element_type=jnp.float32
    )
    incoming = shifted(window_grad[-1, STRIDE:], "seq", 1)
    carried_grad = jnp.concatenate([incoming[None], window_grad[:-1, STRIDE:]], axis=0)
    byte_grad = (
        (window_grad[:, :STRIDE] + carried_grad).reshape(row_total, width).astype(jnp.bfloat16)
    )
    return (downsampled[None], byte_grad[None], conv_grad, proj_grad)


def solution(mesh):
    return jax.shard_map(
        local,
        mesh=mesh,
        in_specs=(
            P("dp", "seq", "tensor"),
            P("tensor", None, None),
            P("tensor"),
            P(None, "tensor"),
            P("dp", "seq", "tensor"),
            P("dp", None),
        ),
        out_specs=(
            P("dp", "seq", "tensor"),
            P("dp", "seq", "tensor"),
            P("tensor", None, None),
            P(None, "tensor"),
        ),
        check_vma=False,
    )
```

profile of v0, /device:TPU:1, one launch (start us, length us, event | category | flops | bytes accessed | tf_op | source)
XLA Modules:
  0.0 448.6 jit_solution(9548664783384587583)
XLA Ops:
  7.2 0.8 slice_bitcast_fusion
  8.1 5.1 %collective-permute-start = (bf16[4,128]{1,0:T(4,128)(2,1)S(1)}, bf16[4,128]{1,0:T(4,128)(2,1)S(1)}, u32[]{:S(2)}, u32[]{:S(2)}) collective-permute-start(bf16[4,128]{1,0:T(4,128)(2,1)S(1)} %slice_bitcast_fusion), channel_id=1, source_target_pairs={{16,0},{32,16},{48,32},{17,1},{33,17},{49,33},{18,2},{34,18},{50,3... | collective-permute-start | bytes 3080 | tf_op jit(solution)/shard_map/ppermute | solution.py:13
  13.2 1.0 reduce-window.9
  14.5 0.8 fusion.23
  15.3 0.7 convert_element_type.87
  16.0 1.4 copy.17
  17.4 1.5 pad_maximum_fusion
  19.1 1.0 copy-done.1
  20.0 0.7 fusion.11
  20.8 0.7 copy-done.7
  21.5 7.5 %fusion.2 = bf16[4096,128]{1,0:T(8,128)(2,1)} fusion(f32[4096]{0:T(1024)S(1)} %convert_element_type.87, s32[1024]{0:T(1024)S(1)} %add_multiply_fusion, s32[4096]{0:T(1024)S(1)} %get-tuple-element.6, s32[1024]{0:T(1024)S(1)} %broadcast_add_fusion, s32[4096]{0:T(1024)S(1)} %get-tuple-element.7, bf16[1,128,1024]{1,2,0:T(8,128)(2,1)S(1)} %fusion.11), kind=kOutput, calls=%fused_computation.3 | convolution fusion | flops 1103626240 | bytes 1368064 | tf_op jit(solution)/shard_map/dot_general | solution.py:51
  29.0 38.1 %reduce-scatter.5.cloned.1.call-done = bf16[1024,128]{1,0:T(8,128)(2,1)} async-done(((bf16[4096,128]{1,0:T(8,128)(2,1)}), bf16[1024,128]{1,0:T(8,128)(2,1)}) %reduce-scatter.5.cloned.1.call-update) | async-done | bytes 262160 | tf_op jit(solution)/shard_map/reduce_scatter | solution.py:50
  67.2 80.8 %all-gather.3.cloned.1.call-done = bf16[1024,2048]{1,0:T(8,128)(2,1)} async-done(((bf16[1024,128]{1,0:T(8,128)(2,1)}), bf16[1024,2048]{1,0:T(8,128)(2,1)}) %all-gather.3.cloned.1.call-update) | async-done | bytes 4194320 | tf_op jit(solution)/shard_map/all_gather | solution.py:56
  148.1 4.6 %fusion.24 = f32[1024,512]{1,0:T(8,128)S(1)} fusion(bf16[1024,2048]{1,0:T(8,128)(2,1)} %all-gather.3.cloned.1.call-done, bf16[2048,512]{1,0:T(8,128)(2,1)S(1)} %copy-done), kind=kOutput, calls=%fused_computation.37 | convolution fusion | flops 2147483648 | bytes 8388608 | tf_op jit(solution)/shard_map/dot_general | solution.py:57
  152.7 1.4 copy-done.8
  154.0 4.4 convert_bitcast_fusion
  158.4 6.4 %copy.23 = bf16[2048,1024]{1,0:T(8,128)(2,1)} copy(bf16[2048,1024]{0,1:T(8,128)(2,1)} %convert_bitcast_fusion) | data formatting | bytes 8388608
  164.9 78.6 %reduce-scatter.7.cloned.1.call-done = bf16[128,1024]{1,0:T(8,128)(2,1)} async-done(((bf16[2048,1024]{1,0:T(8,128)(2,1)}), bf16[128,1024]{1,0:T(8,128)(2,1)}) %reduce-scatter.7.cloned.1.call-update) | async-done | bytes 262160
  243.5 1.8 copy.24
  245.6 6.8 %convolution_convert_fusion = bf16[2048,512]{1,0:T(8,128)(2,1)} fusion(bf16[1024,2048]{1,0:T(8,128)(2,1)} %all-gather.3.cloned.1.call-done, f32[1024,512]{1,0:T(8,128)} %copy-done.8, bf16[1,1024,512]{2,1,0:T(8,128)(2,1)} %param.10), kind=kOutput, calls=%fused_computation.6 | convolution fusion | flops 2150105088 | bytes 9437184 | tf_op jit(solution)/shard_map/dot_general | solution.py:59
  252.3 24.2 %all-gather.5.cloned.1.call-done = bf16[128,4096]{0,1:T(8,128)(2,1)} async-done(((bf16[128,1024]{0,1:T(8,128)(2,1)}), bf16[128,4096]{0,1:T(8,128)(2,1)}) %all-gather.5.cloned.1.call-update) | async-done | bytes 1048592 | tf_op jit(solution)/shard_map/all_gather | solution.py:77
  276.5 7.7 %fusion.15 = bf16[1024,128,1]{1,0,2:T(8,128)(2,1)S(1)} fusion(bf16[128,4096]{0,1:T(8,128)(2,1)} %all-gather.5.cloned.1.call-done, f32[4096]{0:T(1024)S(1)} %convert_element_type.87, s32[1024]{0:T(1024)S(1)} %add_multiply_fusion, s32[4096]{0:T(1024)S(1)} %get-tuple-element.6, s32[1024]{0:T(1024)S(1)} %broadcast_add_fusion, s32[4096]{0:T(1024)S(1)} %get-tuple-element.7), kind=kOutput, calls=%fused_computation.21 | convolution fusion | flops 1103233024 | bytes 1368064 | tf_op jit(solution)/shard_map/dot_general | solution.py:75
  284.2 0.7 copy-done.4
  284.9 1.4 fusion.14
  286.4 1.7 convolution_bitcast_fusion
  288.1 2.1 collective-permute-start.1
  290.3 0.8 collective-permute-done.1
  291.1 0.3 fusion.3
  291.4 1.8 copy.20
  293.2 142.9 %all-reduce.3.cloned.1.call-done = (bf16[1,8,128,128]{3,2,1,0:T(8,128)(2,1)}, bf16[2048,512]{1,0:T(8,128)(2,1)}) async-done(((bf16[1,8,128,128]{3,2,1,0:T(8,128)(2,1)}, bf16[2048,512]{1,0:T(8,128)(2,1)}), (bf16[1,8,128,128]{3,2,1,0:T(8,128)(2,1)}, bf16[2048,512]{1,0:T(8,128)(2,1)})) %all-reduce.3.cloned.1.call-update) | async-done | bytes 2359312 | tf_op jit(solution)/shard_map/psum | solution.py:85
  436.1 1.8 convert_multiply_fusion.1
  437.9 4.2 convert_multiply_fusion
  (33 shorter events, 1.0 us)
Async XLA Ops:
  7.2 140.9 %copy-start = (bf16[2048,512]{1,0:T(8,128)(2,1)S(1)}, bf16[2048,512]{1,0:T(8,128)(2,1)}, u32[]{:S(2)}) copy-start(bf16[2048,512]{1,0:T(8,128)(2,1)} %param.9) | copy-start | bytes 6291460
  7.2 12.8 %copy-start.6 = (f32[128]{0:T(128)S(1)}, f32[128]{0:T(128)}, u32[]{:S(2)}) copy-start(f32[128]{0:T(128)} %param.8) | copy-start | bytes 1540
  7.2 12.8 %copy-start.3 = (bf16[1,1024,128]{2,1,0:T(8,128)(2,1)S(1)}, bf16[1,1024,128]{2,1,0:T(8,128)(2,1)}, u32[]{:S(2)}) copy-start(bf16[1,1024,128]{2,1,0:T(8,128)(2,1)} %param.7) | copy-start | bytes 786436
  7.2 60.0 %reduce-scatter.5.cloned.1.call-start = ((), (), s32[]{:S(2)}) async-start(), calls=%async_computation.2 | async-start | bytes 1310720 | tf_op jit(solution)/shard_map/reduce_scatter | solution.py:50
  8.1 9.3 %collective-permute-start = (bf16[4,128]{1,0:T(4,128)(2,1)S(1)}, bf16[4,128]{1,0:T(4,128)(2,1)S(1)}, u32[]{:S(2)}, u32[]{:S(2)}) collective-permute-start(bf16[4,128]{1,0:T(4,128)(2,1)S(1)} %slice_bitcast_fusion), channel_id=1, source_target_pairs={{16,0},{32,16},{48,32},{17,1},{33,17},{49,33},{18,2},{34,18},{50,3... | collective-permute-start | bytes 3080 | tf_op jit(solution)/shard_map/ppermute | solution.py:13
  19.0 1.0 copy-start.1
  20.7 0.7 copy-start.7
  29.0 119.1 %all-gather.3.cloned.1.call-start = ((), (), s32[]{:S(2)}) async-start(), calls=%async_computation.3 | async-start | bytes 4456448 | tf_op jit(solution)/shard_map/all_gather | solution.py:56
  67.2 176.3 %reduce-scatter.7.cloned.1.call-start = ((), (), s32[]{:S(2)}) async-start(), calls=%async_computation.5 | async-start | bytes 4456448
  148.1 6.0 %copy-start.5 = (bf16[1,1024,512]{2,1,0:T(8,128)(2,1)S(1)}, bf16[1,1024,512]{2,1,0:T(8,128)(2,1)}, u32[]{:S(2)}) copy-start(bf16[1,1024,512]{2,1,0:T(8,128)(2,1)} %param.10) | copy-start | bytes 3145732
  152.7 1.4 copy-start.8
  164.9 111.6 %all-gather.5.cloned.1.call-start = ((), (), s32[]{:S(2)}) async-start(), calls=%async_computation.4 | async-start | bytes 1310720 | tf_op jit(solution)/shard_map/all_gather | solution.py:77
  245.3 190.8 %all-reduce.3.cloned.1.call-start = ((), (), s32[]{:S(2)}) async-start(), calls=%async_computation.6 | async-start | bytes 4718592 | tf_op jit(solution)/shard_map/psum | solution.py:85
  276.5 8.4 %copy-start.2 = (bf16[1024,4,1,128]{3,0,1,2:T(8,128)(2,1)S(1)}, bf16[1024,4,1,128]{3,0,1,2:T(8,128)(2,1)}, u32[]{:S(2)}) copy-start(bf16[1024,4,1,128]{3,0,1,2:T(8,128)(2,1)} %copy-done.1) | copy-start | bytes 3145732
  284.2 0.7 copy-start.4
  288.1 3.1 collective-permute-start.1
Sparse Core Ops, SparseCore 0:
  29.1 38.0 reduce-scatter.4
  69.0 79.0 all-gather.2
  165.0 78.4 reduce-scatter.6
  245.9 30.5 all-gather.4
  286.5 149.5 all-reduce.2
where the time goes:
time: 449 us
  waiting for transfers between devices  366 us (82%)
  matrix products  34.8 us (8%)
  local copies, waits for them, and re-layouts  16.4 us (4%)
  between operations  13.9 us (3%)
  other arithmetic  10.3 us (2%)
  starting transfers between devices  7.58 us (2%)
    psum x1, waiting for transfers between devices, local(): lax.psum(conv_local.astype(jnp.bfloat16), ('dp', 'seq')).astype(jnp.float32)  143 us
    all_gather x1, waiting for transfers between devices, local(): gathered = lax.all_gather(pooled_sum, 'tensor', axis=1, tiled=True)  80.8 us
    unnamed x6, waiting for transfers between devices  78.7 us
    reduce_scatter x1, waiting for transfers between devices, local(): lax.psum_scatter(jnp.dot(weight_part, downsampled, preferred_element_type...  38.1 us
    all_gather x1, waiting for transfers between devices, local(): lax.all_gather(pooled_grad_t, 'seq', axis=1, tiled=True)  24.2 us
    unnamed x20, local copies, waits for them, and re-layouts  12 us
  transfers between devices with their start and end apart: 7, of which 6 were waited for; matrix products, arithmetic and copies ran while one was open for 3% of the time, Pallas kernels for 0%

commit v1 on v0

--- a/solution.py
+++ b/solution.py
@@ -82,7 +82,8 @@
     conv_local = jnp.einsum(
         "pkgc,pgo->gkco", windows, down_grad, preferred_element_type=jnp.float32
     )
-    conv_summed = lax.psum(conv_local.astype(jnp.bfloat16), ("dp", "seq")).astype(jnp.float32)
+    detail_groups = lambda xx, chip_axis: jnp.sum(lax.all_gather(xx, chip_axis), axis=0)
+    conv_summed = detail_groups(conv_local.astype(jnp.bfloat16), ("dp", "seq")).astype(jnp.float32)
     position_scale = 1.0 / jnp.sqrt(jnp.float32(lax.axis_size("dp") * positions * seq_count))
     conv_grad = (conv_summed * position_scale).reshape(
         groups_here, KERNEL * group_width, group_width

time: 449 us -> 505 us (1.12)
  waiting for transfers between devices: 366 us -> 417 us
    all_gather x0 -> x1, waiting for transfers between devices: none -> 59.2 us  [local(): lax.all_gather(xx, chip_axis)]
    psum x1, waiting for transfers between devices: 143 us -> 136 us  [local(): lax.psum(proj_local.astype(jnp.bfloat16), ('dp', 'seq')).astype(jnp.float32)]
    unnamed x20 -> x24, local copies, waits for them, and re-layouts: 12 us -> 13.9 us
    unnamed x6 -> x7, waiting for transfers between devices: 78.7 us -> 78.7 us
  transfers between devices with their start and end apart: 7 -> 8, of which waited for: 6 -> 6; matrix products, arithmetic and copies ran while one was open for 3% -> 6% of each run, Pallas kernels for 0% -> 0%
where the time goes in v1:
time: 505 us; the launch traced here: 504 us
  waiting for transfers between devices  417 us (83%)
  matrix products  34.8 us (7%)
  local copies, waits for them, and re-layouts  18.4 us (4%)
  between operations  14.3 us (3%)
  other arithmetic  12.5 us (2%)
  starting transfers between devices  7.61 us (2%)
    psum x1, waiting for transfers between devices, local(): lax.psum(proj_local.astype(jnp.bfloat16), ('dp', 'seq')).astype(jnp.float32)  136 us
    all_gather x1, waiting for transfers between devices, local(): gathered = lax.all_gather(pooled_sum, 'tensor', axis=1, tiled=True)  80.8 us
    unnamed x7, waiting for transfers between devices  78.7 us
    all_gather x1, waiting for transfers between devices, local(): lax.all_gather(xx, chip_axis)  59.2 us
    reduce_scatter x1, waiting for transfers between devices, local(): lax.psum_scatter(jnp.dot(weight_part, downsampled, preferred_element_type...  38.1 us
    all_gather x1, waiting for transfers between devices, local(): lax.all_gather(pooled_grad_t, 'seq', axis=1, tiled=True)  24.1 us
    unnamed x24, local copies, waits for them, and re-layouts  13.9 us
  transfers between devices with their start and end apart: 8, of which 6 were waited for; matrix products, arithmetic and copies ran while one was open for 6% of the time, Pallas kernels for 0%

profile of v1, /device:TPU:1, one launch (start us, length us, event | category | flops | bytes accessed | tf_op | source)
XLA Modules:
  0.0 504.5 jit_solution(6166291398364459517)
XLA Ops:
  7.2 0.8 slice_bitcast_fusion
  8.1 5.1 %collective-permute-start = (bf16[4,128]{1,0:T(4,128)(2,1)S(1)}, bf16[4,128]{1,0:T(4,128)(2,1)S(1)}, u32[]{:S(2)}, u32[]{:S(2)}) collective-permute-start(bf16[4,128]{1,0:T(4,128)(2,1)S(1)} %slice_bitcast_fusion), channel_id=1, source_target_pairs={{16,0},{32,16},{48,32},{17,1},{33,17},{49,33},{18,2},{34,18},{50,3... | collective-permute-start | bytes 3080 | tf_op jit(solution)/shard_map/ppermute | solution.py:13
  13.2 1.0 reduce-window.9
  14.5 0.8 fusion.22
  15.3 0.7 convert_element_type.97
  16.0 1.4 copy.17
  17.4 1.5 pad_maximum_fusion
  19.1 1.0 copy-done.3
  20.0 0.7 fusion.11
  20.8 0.7 copy-done.9
  21.5 7.5 %fusion.2 = bf16[4096,128]{1,0:T(8,128)(2,1)} fusion(f32[4096]{0:T(1024)S(1)} %convert_element_type.97, s32[1024]{0:T(1024)S(1)} %add_multiply_fusion, s32[4096]{0:T(1024)S(1)} %get-tuple-element.4, s32[1024]{0:T(1024)S(1)} %broadcast_add_fusion, s32[4096]{0:T(1024)S(1)} %get-tuple-element.5, bf16[1,128,1024]{1,2,0:T(8,128)(2,1)S(1)} %fusion.11), kind=kOutput, calls=%fused_computation.3 | convolution fusion | flops 1103626240 | bytes 1368064 | tf_op jit(solution)/shard_map/dot_general | solution.py:51
  29.0 38.1 %reduce-scatter.5.cloned.1.call-done = bf16[1024,128]{1,0:T(8,128)(2,1)} async-done(((bf16[4096,128]{1,0:T(8,128)(2,1)}), bf16[1024,128]{1,0:T(8,128)(2,1)}) %reduce-scatter.5.cloned.1.call-update) | async-done | bytes 262160 | tf_op jit(solution)/shard_map/reduce_scatter | solution.py:50
  67.2 80.8 %all-gather.5.cloned.1.call-done = bf16[1024,2048]{1,0:T(8,128)(2,1)} async-done(((bf16[1024,128]{1,0:T(8,128)(2,1)}), bf16[1024,2048]{1,0:T(8,128)(2,1)}) %all-gather.5.cloned.1.call-update) | async-done | bytes 4194320 | tf_op jit(solution)/shard_map/all_gather | solution.py:56
  148.1 4.6 fusion.23
  152.7 1.4 copy-done.10
  154.0 4.4 convert_bitcast_fusion
  158.4 6.4 %copy.23 = bf16[2048,1024]{1,0:T(8,128)(2,1)} copy(bf16[2048,1024]{0,1:T(8,128)(2,1)} %convert_bitcast_fusion) | data formatting | bytes 8388608
  164.9 78.6 %reduce-scatter.7.cloned.1.call-done = bf16[128,1024]{1,0:T(8,128)(2,1)} async-done(((bf16[2048,1024]{1,0:T(8,128)(2,1)}), bf16[128,1024]{1,0:T(8,128)(2,1)}) %reduce-scatter.7.cloned.1.call-update) | async-done | bytes 262160
  243.5 1.8 copy.24
  245.4 6.8 %convolution_convert_fusion = bf16[2048,512]{1,0:T(8,128)(2,1)} fusion(bf16[1024,2048]{1,0:T(8,128)(2,1)} %all-gather.5.cloned.1.call-done, f32[1024,512]{1,0:T(8,128)} %copy-done.10, bf16[1,1024,512]{2,1,0:T(8,128)(2,1)} %param.10), kind=kOutput, calls=%fused_computation.6 | convolution fusion | flops 2150105088 | bytes 9437184 | tf_op jit(solution)/shard_map/dot_general | solution.py:59
  252.4 24.1 %all-gather.7.cloned.1.call-done = bf16[128,4096]{0,1:T(8,128)(2,1)} async-done(((bf16[128,1024]{0,1:T(8,128)(2,1)}), bf16[128,4096]{0,1:T(8,128)(2,1)}) %all-gather.7.cloned.1.call-update) | async-done | bytes 1048592 | tf_op jit(solution)/shard_map/all_gather | solution.py:77
  276.5 7.7 %fusion.14 = bf16[1024,128,1]{1,0,2:T(8,128)(2,1)S(1)} fusion(bf16[128,4096]{0,1:T(8,128)(2,1)} %all-gather.7.cloned.1.call-done, f32[4096]{0:T(1024)S(1)} %convert_element_type.97, s32[1024]{0:T(1024)S(1)} %add_multiply_fusion, s32[4096]{0:T(1024)S(1)} %get-tuple-element.4, s32[1024]{0:T(1024)S(1)} %broadcast_add_fusion, s32[4096]{0:T(1024)S(1)} %get-tuple-element.5), kind=kOutput, calls=%fused_computation.20 | convolution fusion | flops 1103233024 | bytes 1368064 | tf_op jit(solution)/shard_map/dot_general | solution.py:75
  284.9 1.5 fusion.12
  286.4 1.7 convolution_bitcast_fusion
  288.1 2.0 copy-done.1
  290.0 2.1 collective-permute-start.1
  292.1 135.9 %all-reduce.2.cloned.1.call-done = bf16[2048,512]{1,0:T(8,128)(2,1)} async-done(((bf16[2048,512]{1,0:T(8,128)(2,1)}), bf16[2048,512]{1,0:T(8,128)(2,1)}) %all-reduce.2.cloned.1.call-update) | async-done | bytes 2097168 | tf_op jit(solution)/shard_map/psum | solution.py:63
  428.0 4.3 convert_multiply_fusion
  432.8 1.8 copy.20
  434.6 59.2 %all-gather.9.cloned.1.call-done = bf16[128,128,128]{2,1,0:T(8,128)(2,1)} async-done(((bf16[8,128,128]{2,1,0:T(8,128)(2,1)}), bf16[128,128,128]{2,1,0:T(8,128)(2,1)}) %all-gather.9.cloned.1.call-update) | async-done | bytes 4194320 | tf_op jit(solution)/shard_map/all_gather | solution.py:85
  493.8 3.0 reduce.2
  496.8 0.8 convert_multiply_fusion.1
  (41 shorter events, 2.1 us)
Async XLA Ops:
  7.2 140.9 %copy-start = (bf16[2048,512]{1,0:T(8,128)(2,1)S(1)}, bf16[2048,512]{1,0:T(8,128)(2,1)}, u32[]{:S(2)}) copy-start(bf16[2048,512]{1,0:T(8,128)(2,1)} %param.9) | copy-start | bytes 6291460
  7.2 12.8 %copy-start.8 = (f32[128]{0:T(128)S(1)}, f32[128]{0:T(128)}, u32[]{:S(2)}) copy-start(f32[128]{0:T(128)} %param.8) | copy-start | bytes 1540
  7.2 12.8 %copy-start.5 = (bf16[1,1024,128]{2,1,0:T(8,128)(2,1)S(1)}, bf16[1,1024,128]{2,1,0:T(8,128)(2,1)}, u32[]{:S(2)}) copy-start(bf16[1,1024,128]{2,1,0:T(8,128)(2,1)} %param.7) | copy-start | bytes 786436
  7.2 60.0 %reduce-scatter.5.cloned.1.call-start = ((), (), s32[]{:S(2)}) async-start(), calls=%async_computation.2 | async-start | bytes 1310720 | tf_op jit(solution)/shard_map/reduce_scatter | solution.py:50
  8.1 9.3 %collective-permute-start = (bf16[4,128]{1,0:T(4,128)(2,1)S(1)}, bf16[4,128]{1,0:T(4,128)(2,1)S(1)}, u32[]{:S(2)}, u32[]{:S(2)}) collective-permute-start(bf16[4,128]{1,0:T(4,128)(2,1)S(1)} %slice_bitcast_fusion), channel_id=1, source_target_pairs={{16,0},{32,16},{48,32},{17,1},{33,17},{49,33},{18,2},{34,18},{50,3... | collective-permute-start | bytes 3080 | tf_op jit(solution)/shard_map/ppermute | solution.py:13
  19.0 1.0 copy-start.3
  20.7 0.7 copy-start.9
  29.0 119.1 %all-gather.5.cloned.1.call-start = ((), (), s32[]{:S(2)}) async-start(), calls=%async_computation.3 | async-start | bytes 4456448 | tf_op jit(solution)/shard_map/all_gather | solution.py:56
  67.2 176.3 %reduce-scatter.7.cloned.1.call-start = ((), (), s32[]{:S(2)}) async-start(), calls=%async_computation.7 | async-start | bytes 4456448
  148.1 6.0 %copy-start.7 = (bf16[1,1024,512]{2,1,0:T(8,128)(2,1)S(1)}, bf16[1,1024,512]{2,1,0:T(8,128)(2,1)}, u32[]{:S(2)}) copy-start(bf16[1,1024,512]{2,1,0:T(8,128)(2,1)} %param.10) | copy-start | bytes 3145732
  152.7 1.4 copy-start.10
  164.9 111.6 %all-gather.7.cloned.1.call-start = ((), (), s32[]{:S(2)}) async-start(), calls=%async_computation.4 | async-start | bytes 1310720 | tf_op jit(solution)/shard_map/all_gather | solution.py:77
  245.3 182.7 %all-reduce.2.cloned.1.call-start = ((), (), s32[]{:S(2)}) async-start(), calls=%async_computation.5 | async-start | bytes 4194304 | tf_op jit(solution)/shard_map/psum | solution.py:63
  252.2 241.6 %all-gather.9.cloned.1.call-start = ((), (), s32[]{:S(2)}) async-start(), calls=%async_computation.6 | async-start | bytes 4456448 | tf_op jit(solution)/shard_map/all_gather | solution.py:85
  276.5 8.4 %copy-start.4 = (bf16[1024,4,1,128]{3,0,1,2:T(8,128)(2,1)S(1)}, bf16[1024,4,1,128]{3,0,1,2:T(8,128)(2,1)}, u32[]{:S(2)}) copy-start(bf16[1024,4,1,128]{3,0,1,2:T(8,128)(2,1)} %copy-done.3) | copy-start | bytes 3145732
  284.2 0.7 copy-start.6
  288.1 2.0 copy-start.1
  290.0 142.5 %collective-permute-start.1 = (f32[4,1,128]{2,0,1:T(4,128)S(1)}, f32[4,1,128]{2,0,1:T(4,128)S(1)}, u32[]{:S(2)}, u32[]{:S(2)}) collective-permute-start(f32[4,1,128]{2,0,1:T(4,128)S(1)} %bitcast.89), channel_id=1, source_target_pairs={{0,16},{16,32},{32,48},{1,17},{17,33},{33,49},{2,18},{18,34},{34,5... | collective-permute-start | bytes 6152 | tf_op jit(solution)/shard_map/ppermute | solution.py:13
  428.0 4.4 copy-start.2
Sparse Core Ops, SparseCore 0:
  29.1 38.0 reduce-scatter.4
  69.0 79.0 all-gather.4
  165.0 78.4 reduce-scatter.6
  245.9 30.5 all-gather.6
  279.8 148.2 all-reduce.1
  430.9 62.8 all-gather.8
